TPU v7x, 128 devices: a whole 4x4x4 slice. The times are simulated.
128 devices in a mesh: tok: 32 (over z, x, core), head: 4 (over y).
Axes of the slice: x: 4, y: 4, z: 4, core: 2. Of those that a mesh axis runs over, the one named last changes fastest.
Arguments:
- hidden_in: bfloat16 [32, 512, 5120], P('tok', None, 'head')
- norm_gain: float32 [5120], replicated, may hold values from 0.1 to 1.9
- w_query: bfloat16 [5120, 2048], P(None, 'head'), may hold values from -0.078125 to 0.078125
- w_key: bfloat16 [5120, 512], P(None, 'head'), may hold values from -0.15625 to 0.15625
- w_value: bfloat16 [5120, 512], P(None, 'head'), may hold values from -0.078125 to 0.078125
- w_out: bfloat16 [2048, 5120], P(None, 'head'), may hold values from -0.5 to 0.5
- prefix_cache: bfloat16 [64, 2, 128, 512], P('tok', None, None, 'head')
- suffix_len: int32 [32], replicated, may hold values from 1 to 512, 10240 in all
- page_table: int32 [2, 32], replicated, may hold values from 0 to 63, as said below
- request_group: int32 [32], replicated, may hold values from 0 to 1, as said below
Outputs:
- hidden_out: bfloat16 [32, 512, 5120], P('tok', None, 'head')
Inputs may be any that keep to these rules, and one draw needn't show every extreme that they name: `page_table`: every one of the 64 slots appears exactly once; row g lists the slots that hold group g's prefix pages, page by page. `request_group`: exactly half of the 32 requests are in each group.
All inputs are finite; a program needn't handle non-finite values.
Results may differ from a plain program's by a relative error of at most 0.008.
The roundings to bfloat16 on the way count: a program that leaves them out, or rounds other values in their place, can miss the bound.
Values may be sent and summed in bfloat16 or wider, within the bound.
No kernel may reach another device: no remote copies, remote signals or barrier semaphores. Data moves between devices by JAX's collectives and lax.ppermute only.
A program may use at most 128 MiB of HBM per device.

v0:
```python
import math
import jax
import jax.numpy as jnp
from jax import lax
from jax.sharding import PartitionSpec as P

HD = 128
PREFIX = 4096
THETA = 100000000.0
EPS = 1e-05
NEG = -1e30


def rope_angles(positions, size):
    half = size // 2
    ladder = jnp.arange(half, dtype=jnp.float32)
    freq = jnp.exp(ladder * (-2.0 * jnp.log(THETA) / size))
    angle = positions.astype(jnp.float32)[:, None] * freq[None, :]
    return (jnp.cos(angle), jnp.sin(angle))


def rotate(values, cosine, sine):
    half = values.shape[-1] // 2
    first = values[..., :half]
    second = values[..., half:]
    return jnp.concatenate(
        [first * cosine - second * sine, second * cosine + first * sine], axis=-1
    )


def online_block(carry, queries, block_keys, block_values, allowed):
    highest, total, numerator = carry
    scores = lax.dot_general(
        queries, block_keys, (((1,), (1,)), ((), ())), preferred_element_type=jnp.float32
    )
    scores = jnp.where(allowed, scores * queries.shape[1] ** (-0.5), NEG)
    new_high = jnp.maximum(highest, jnp.max(scores, axis=1))
    weights = jnp.where(allowed, jnp.exp(scores - new_high[:, None]), 0.0)
    factor = jnp.exp(highest - new_high)
    total = total * factor + jnp.sum(weights, axis=1)
    numerator = numerator * factor[:, None] + jnp.dot(
        weights.astype(jnp.bfloat16), block_values, preferred_element_type=jnp.float32
    )
    return (new_high, total, numerator)


def fold_keys(carry, queries, all_keys, all_values, allowed):
    count = all_keys.shape[0]
    block = math.gcd(count, 512)
    rounds = count // block
    if rounds == 1:
        return online_block(carry, queries, all_keys, all_values, allowed)
    key_blocks = all_keys.reshape(rounds, block, all_keys.shape[1])
    value_blocks = all_values.reshape(rounds, block, all_values.shape[1])
    mask_blocks = allowed.reshape(allowed.shape[0], rounds, block).transpose(1, 0, 2)

    def advance(state, items):
        return (online_block(state, queries, items[0], items[1], items[2]), None)

    carry, _ = lax.scan(advance, carry, (key_blocks, value_blocks, mask_blocks))
    return carry


def local(
    hidden_in,
    norm_gain,
    w_query,
    w_key,
    w_value,
    w_out,
    prefix_cache,
    suffix_len,
    page_table,
    request_group,
):
    local_len = hidden_in.shape[1]
    whole = lax.all_gather(hidden_in, "head", axis=2, tiled=True)
    flat = whole.reshape(local_len, whole.shape[2]).astype(jnp.float32)
    inverse = lax.rsqrt(jnp.mean(flat * flat, axis=1, keepdims=True) + EPS)
    normed = (flat * inverse * norm_gain[None, :]).astype(jnp.bfloat16)
    head_size = HD
    kv_local = w_key.shape[1] // head_size
    q_local = w_query.shape[1] // head_size
    per_kv = q_local // kv_local
    device = lax.axis_index("tok")
    positions = PREFIX + jnp.arange(local_len, dtype=jnp.int32)
    cosine, sine = rope_angles(positions, head_size)
    cosine = cosine[:, None, :]
    sine = sine[:, None, :]
    query = jnp.dot(normed, w_query, preferred_element_type=jnp.float32).reshape(
        local_len, q_local, head_size
    )
    query = rotate(query, cosine, sine).astype(jnp.bfloat16)
    keys = jnp.dot(normed, w_key, preferred_element_type=jnp.float32).reshape(
        local_len, kv_local, head_size
    )
    keys = rotate(keys, cosine, sine).astype(jnp.bfloat16)
    values = jnp.dot(normed, w_value, preferred_element_type=jnp.float32).astype(jnp.bfloat16)
    values = values.reshape(local_len, kv_local, head_size)
    length = suffix_len[device]
    group = request_group[device]
    own_pages = page_table[group]
    total_rows = per_kv * local_len
    q_rows = [query.transpose(1, 0, 2).reshape(total_rows, head_size)]
    start_state = (
        jnp.full((total_rows,), NEG, jnp.float32),
        jnp.zeros((total_rows,), jnp.float32),
        jnp.zeros((total_rows, head_size), jnp.float32),
    )
    carry = tuple((start_state for k in range(kv_local)))
    piece = lax.all_gather(prefix_cache, "tok", axis=0, tiled=True)
    count = piece.shape[0]
    slots = jnp.arange(count, dtype=jnp.int32)
    member = jnp.any(own_pages[:, None] == slots[None, :], axis=0)
    allowed = jnp.repeat(member, piece.shape[2])[None, :]
    k = 0
    page_keys = piece[:, 0].reshape(count * piece.shape[2], head_size)
    page_values = piece[:, 1].reshape(count * piece.shape[2], head_size)
    updated = [fold_keys(carry[k], q_rows[k], page_keys, page_values, allowed)]
    carry = tuple(updated)
    query_pos = jnp.arange(total_rows, dtype=jnp.int32) % local_len
    key_pos = jnp.arange(local_len, dtype=jnp.int32)
    causal = (key_pos[None, :] <= query_pos[:, None]) & (key_pos[None, :] < length)
    k = 0
    _, total, numerator = fold_keys(carry[k], q_rows[k], keys[:, k, :], values[:, k, :], causal)
    mixed = (numerator / total[:, None]).astype(jnp.bfloat16)
    pieces = (
        mixed.reshape(per_kv, local_len, head_size)
        .transpose(1, 0, 2)
        .reshape(local_len, per_kv * head_size)
    )
    output = jnp.dot(
        lax.all_gather(pieces, "head", axis=1, tiled=True),
        w_out,
        preferred_element_type=jnp.float32,
    )
    live = jnp.arange(local_len, dtype=jnp.int32) < length
    output = jnp.where(live[:, None], output, 0.0).astype(jnp.bfloat16)
    return output.reshape(1, local_len, w_out.shape[1])


def solution(mesh):
    return jax.shard_map(
        local,
        mesh=mesh,
        in_specs=(
            P("tok", None, "head"),
            P(),
            P(None, "head"),
            P(None, "head"),
            P(None, "head"),
            P(None, "head"),
            P("tok", None, None, "head"),
            P(),
            P(),
            P(),
        ),
        out_specs=P("tok", None, "head"),
        check_vma=False,
    )
```

profile of v0, /device:TPU:1, one launch (start us, length us, event | category | flops | bytes accessed | tf_op | source)
XLA Modules:
  0.0 274.4 jit_solution(10157303807104072718)
XLA Ops:
  13.7 7.8 %copy.24 = bf16[512,5120]{1,0:T(8,128)(2,1)} copy(bf16[512,5120]{0,1:T(8,128)(2,1)} %bitcast.70) | data formatting | bytes 10485760 | tf_op jit(solution)/shard_map/dot_general | solution.py:90
  22.8 46.2 %all-gather.6.cloned.1.call-done = bf16[1,512,5120]{2,1,0:T(8,128)(2,1)} async-done(((bf16[1,512,1280]{2,1,0:T(8,128)(2,1)}), bf16[1,512,5120]{2,1,0:T(8,128)(2,1)}) %all-gather.6.cloned.1.call-update) | async-done | bytes 5242896 | tf_op jit(solution)/shard_map/all_gather | solution.py:77
  69.0 3.7 %fusion.21 = f32[512]{0:T(512)S(1)} fusion(bf16[1,512,5120]{2,1,0:T(8,128)(2,1)} %all-gather.6.cloned.1.call-done), kind=kLoop, calls=%fused_computation.30 | loop fusion | flops 7863808 | bytes 5244928 | tf_op jit(solution)/shard_map/reduce_sum | solution.py:79
  73.0 5.7 %fusion.27 = f32[512,4,128]{0,2,1:T(8,128)S(1)} fusion(bf16[4,128,5120]{2,1,0:T(8,128)(2,1)} %bitcast.71, bf16[1,512,5120]{2,1,0:T(8,128)(2,1)S(1)} %copy-done.1, f32[5120]{0:T(1024)S(1)} %copy-done.2, f32[512]{0:T(512)S(1)} %add_rsqrt_fusion), kind=kOutput, calls=%fused_computation.36 | convolution fusion | flops 2694840320 | bytes 11556864 | tf_op jit(solution)/shard_map/dot_general | solution.py:90
  79.3 4.9 %fusion.46 = f32[512,1,128]{0,2,1:T(8,128)S(1)} fusion(bf16[5120,128]{1,0:T(8,128)(2,1)} %param.15, bf16[1,512,5120]{2,1,0:T(8,128)(2,1)} %all-gather.6.cloned.1.call-done, f32[5120]{0:T(1024)S(1)} %copy-done.2, f32[512]{0:T(512)S(1)} %add_rsqrt_fusion), kind=kOutput, calls=%fused_computation.56 | convolution fusion | flops 681574400 | bytes 6838272 | tf_op jit(solution)/shard_map/dot_general | solution.py:94
  84.7 3.3 %fusion.74 = (f32[2048]{0:T(1024)S(1)}, f32[2048,512]{0,1:T(8,128)}) fusion(bf16[2048,128]{1,0:T(8,128)(2,1)S(1)} %bitcast.68, bf16[512,64]{0,1:T(8,128)(2,1)S(1)} %get-tuple-element.130, bf16[512,64]{0,1:T(8,128)(2,1)S(1)} %get-tuple-element.129, pred[512]{0:T(512)(128)(4,1)S(1)} %iota_compare_fusion.2, s32[2048]{0:T(1024)S(1)} %add_select_fusion), kind=kOutput, calls=%fused_computation.95 | convolution fusion | flops 273938432 | bytes 4866560 | tf_op jit(solution)/shard_map/dot_general | solution.py:33
  88.1 30.4 %all-gather.4.cloned.1.call-done = bf16[64,2,128,128]{3,2,1,0:T(8,128)(2,1)} async-done(((bf16[2,2,128,128]{3,2,1,0:T(8,128)(2,1)}), bf16[64,2,128,128]{3,2,1,0:T(8,128)(2,1)}) %all-gather.4.cloned.1.call-update) | async-done | bytes 4194320 | tf_op jit(solution)/shard_map/all_gather | solution.py:111
  118.5 4.9 %fusion.73 = (bf16[64,1,128,128]{3,2,1,0:T(8,128)(2,1)}, bf16[64,1,128,128]{3,2,1,0:T(8,128)(2,1)}) fusion(bf16[64,2,128,128]{3,2,1,0:T(8,128)(2,1)} %all-gather.4.cloned.1.call-done), kind=kLoop, calls=%fused_computation.94 | loop fusion | bytes 8388608 | tf_op jit(solution)/shard_map/slice | solution.py:118
  123.4 95.6 %while.15 = (s32[]{:T(128)}, f32[2048]{0:T(1024)S(1)}, f32[2048]{0:T(1024)S(1)}, f32[2048,128]{1,0:T(8,128)S(1)}, pred[16,1,512]{2,1,0:T(4,128)(4,1)S(1)}, /*ind...) while((s32[]{:T(128)}, f32[2048]{0:T(1024)S(1)}, ...), condition=%wide.region_5.6_spmd.clone, body=%wide.region_2.5_spmd.clone.sunk | while | flops 551299072 | bytes 15600261 | solution.py:60
  126.4 2.9 %convolution_add_fusion.3 = f32[2048,128]{1,0:T(8,128)S(1)} fusion(f32[512,2048]{1,0:T(8,128)S(1)} %get-tuple-element.189, f32[2048]{0:T(1024)S(1)} %select_maximum_fusion.2, pred[512]{0:T(512)(128)(4,1)S(1)} %dynamic-slice_reduce_fusion.2, f32[2048,128]{1,0:T(8,128)S(1)} %get-tuple-element.205, f32[2048]{0:T(1024)S(1)} %get-tuple-element.191, ...), kind=kOutput, calls=%fused_computation.5.clone.1 | convolution fusion | flops 274464768 | bytes 6439429 | tf_op jit(solution)/shard_map/while/body/eval_jaxpr/dot_general | solution.py:41
  132.3 2.9 %convolution_add_fusion.3 = f32[2048,128]{1,0:T(8,128)S(1)} fusion(f32[512,2048]{1,0:T(8,128)S(1)} %get-tuple-element.189, f32[2048]{0:T(1024)S(1)} %select_maximum_fusion.2, pred[512]{0:T(512)(128)(4,1)S(1)} %dynamic-slice_reduce_fusion.2, f32[2048,128]{1,0:T(8,128)S(1)} %get-tuple-element.205, f32[2048]{0:T(1024)S(1)} %get-tuple-element.191, ...), kind=kOutput, calls=%fused_computation.5.clone.1 | convolution fusion | flops 274464768 | bytes 6439429 | tf_op jit(solution)/shard_map/while/body/eval_jaxpr/dot_general | solution.py:41
  138.3 2.9 %convolution_add_fusion.3 = f32[2048,128]{1,0:T(8,128)S(1)} fusion(f32[512,2048]{1,0:T(8,128)S(1)} %get-tuple-element.189, f32[2048]{0:T(1024)S(1)} %select_maximum_fusion.2, pred[512]{0:T(512)(128)(4,1)S(1)} %dynamic-slice_reduce_fusion.2, f32[2048,128]{1,0:T(8,128)S(1)} %get-tuple-element.205, f32[2048]{0:T(1024)S(1)} %get-tuple-element.191, ...), kind=kOutput, calls=%fused_computation.5.clone.1 | convolution fusion | flops 274464768 | bytes 6439429 | tf_op jit(solution)/shard_map/while/body/eval_jaxpr/dot_general | solution.py:41
  144.3 2.9 %convolution_add_fusion.3 = f32[2048,128]{1,0:T(8,128)S(1)} fusion(f32[512,2048]{1,0:T(8,128)S(1)} %get-tuple-element.189, f32[2048]{0:T(1024)S(1)} %select_maximum_fusion.2, pred[512]{0:T(512)(128)(4,1)S(1)} %dynamic-slice_reduce_fusion.2, f32[2048,128]{1,0:T(8,128)S(1)} %get-tuple-element.205, f32[2048]{0:T(1024)S(1)} %get-tuple-element.191, ...), kind=kOutput, calls=%fused_computation.5.clone.1 | convolution fusion | flops 274464768 | bytes 6439429 | tf_op jit(solution)/shard_map/while/body/eval_jaxpr/dot_general | solution.py:41
  150.2 2.9 %convolution_add_fusion.3 = f32[2048,128]{1,0:T(8,128)S(1)} fusion(f32[512,2048]{1,0:T(8,128)S(1)} %get-tuple-element.189, f32[2048]{0:T(1024)S(1)} %select_maximum_fusion.2, pred[512]{0:T(512)(128)(4,1)S(1)} %dynamic-slice_reduce_fusion.2, f32[2048,128]{1,0:T(8,128)S(1)} %get-tuple-element.205, f32[2048]{0:T(1024)S(1)} %get-tuple-element.191, ...), kind=kOutput, calls=%fused_computation.5.clone.1 | convolution fusion | flops 274464768 | bytes 6439429 | tf_op jit(solution)/shard_map/while/body/eval_jaxpr/dot_general | solution.py:41
  156.2 2.9 %convolution_add_fusion.3 = f32[2048,128]{1,0:T(8,128)S(1)} fusion(f32[512,2048]{1,0:T(8,128)S(1)} %get-tuple-element.189, f32[2048]{0:T(1024)S(1)} %select_maximum_fusion.2, pred[512]{0:T(512)(128)(4,1)S(1)} %dynamic-slice_reduce_fusion.2, f32[2048,128]{1,0:T(8,128)S(1)} %get-tuple-element.205, f32[2048]{0:T(1024)S(1)} %get-tuple-element.191, ...), kind=kOutput, calls=%fused_computation.5.clone.1 | convolution fusion | flops 274464768 | bytes 6439429 | tf_op jit(solution)/shard_map/while/body/eval_jaxpr/dot_general | solution.py:41
  162.1 2.9 %convolution_add_fusion.3 = f32[2048,128]{1,0:T(8,128)S(1)} fusion(f32[512,2048]{1,0:T(8,128)S(1)} %get-tuple-element.189, f32[2048]{0:T(1024)S(1)} %select_maximum_fusion.2, pred[512]{0:T(512)(128)(4,1)S(1)} %dynamic-slice_reduce_fusion.2, f32[2048,128]{1,0:T(8,128)S(1)} %get-tuple-element.205, f32[2048]{0:T(1024)S(1)} %get-tuple-element.191, ...), kind=kOutput, calls=%fused_computation.5.clone.1 | convolution fusion | flops 274464768 | bytes 6439429 | tf_op jit(solution)/shard_map/while/body/eval_jaxpr/dot_general | solution.py:41
  168.1 2.9 %convolution_add_fusion.3 = f32[2048,128]{1,0:T(8,128)S(1)} fusion(f32[512,2048]{1,0:T(8,128)S(1)} %get-tuple-element.189, f32[2048]{0:T(1024)S(1)} %select_maximum_fusion.2, pred[512]{0:T(512)(128)(4,1)S(1)} %dynamic-slice_reduce_fusion.2, f32[2048,128]{1,0:T(8,128)S(1)} %get-tuple-element.205, f32[2048]{0:T(1024)S(1)} %get-tuple-element.191, ...), kind=kOutput, calls=%fused_computation.5.clone.1 | convolution fusion | flops 274464768 | bytes 6439429 | tf_op jit(solution)/shard_map/while/body/eval_jaxpr/dot_general | solution.py:41
  174.1 2.9 %convolution_add_fusion.3 = f32[2048,128]{1,0:T(8,128)S(1)} fusion(f32[512,2048]{1,0:T(8,128)S(1)} %get-tuple-element.189, f32[2048]{0:T(1024)S(1)} %select_maximum_fusion.2, pred[512]{0:T(512)(128)(4,1)S(1)} %dynamic-slice_reduce_fusion.2, f32[2048,128]{1,0:T(8,128)S(1)} %get-tuple-element.205, f32[2048]{0:T(1024)S(1)} %get-tuple-element.191, ...), kind=kOutput, calls=%fused_computation.5.clone.1 | convolution fusion | flops 274464768 | bytes 6439429 | tf_op jit(solution)/shard_map/while/body/eval_jaxpr/dot_general | solution.py:41
  180.0 2.9 %convolution_add_fusion.3 = f32[2048,128]{1,0:T(8,128)S(1)} fusion(f32[512,2048]{1,0:T(8,128)S(1)} %get-tuple-element.189, f32[2048]{0:T(1024)S(1)} %select_maximum_fusion.2, pred[512]{0:T(512)(128)(4,1)S(1)} %dynamic-slice_reduce_fusion.2, f32[2048,128]{1,0:T(8,128)S(1)} %get-tuple-element.205, f32[2048]{0:T(1024)S(1)} %get-tuple-element.191, ...), kind=kOutput, calls=%fused_computation.5.clone.1 | convolution fusion | flops 274464768 | bytes 6439429 | tf_op jit(solution)/shard_map/while/body/eval_jaxpr/dot_general | solution.py:41
  186.0 2.9 %convolution_add_fusion.3 = f32[2048,128]{1,0:T(8,128)S(1)} fusion(f32[512,2048]{1,0:T(8,128)S(1)} %get-tuple-element.189, f32[2048]{0:T(1024)S(1)} %select_maximum_fusion.2, pred[512]{0:T(512)(128)(4,1)S(1)} %dynamic-slice_reduce_fusion.2, f32[2048,128]{1,0:T(8,128)S(1)} %get-tuple-element.205, f32[2048]{0:T(1024)S(1)} %get-tuple-element.191, ...), kind=kOutput, calls=%fused_computation.5.clone.1 | convolution fusion | flops 274464768 | bytes 6439429 | tf_op jit(solution)/shard_map/while/body/eval_jaxpr/dot_general | solution.py:41
  218.9 3.6 %fusion.33 = f32[2048]{0:T(1024)S(1)} fusion(f32[2048,512]{0,1:T(8,128)} %get-tuple-element.134, f32[2048]{0:T(1024)S(1)} %max.6, s32[2048]{0:T(1024)S(1)} %add_select_fusion, pred[512]{0:T(512)(128)(4,1)S(1)} %iota_compare_fusion.2), kind=kLoop, calls=%fused_computation.45 | loop fusion | flops 5240832 | bytes 4219392 | tf_op jit(solution)/shard_map/reduce_sum | solution.py:40
  222.6 7.5 %fusion.37 = bf16[2048,128]{1,0:T(8,128)(2,1)S(1)} fusion(f32[2048,512]{0,1:T(8,128)} %get-tuple-element.134, f32[2048]{0:T(1024)S(1)} %max.6, s32[2048]{0:T(1024)S(1)} %add_select_fusion, pred[512]{0:T(512)(128)(4,1)S(1)} %iota_compare_fusion.2, f32[2048,128]{1,0:T(8,128)S(1)} %get-tuple-element.49, bf16[5120,128]{1,0:T(8,128)(2,1)S(1)} %copy-done, ...), kind=kOutput, calls=%fused_computation.50 | convolution fusion | flops 956366848 | bytes 12376576 | tf_op jit(solution)/shard_map/dot_general | solution.py:41
  231.1 29.7 %all-gather.8.cloned.1.call-done = bf16[512,2048]{0,1:T(8,128)(2,1)} async-done(((bf16[512,512]{0,1:T(8,128)(2,1)}), bf16[512,2048]{0,1:T(8,128)(2,1)}) %all-gather.8.cloned.1.call-update) | async-done | bytes 2097168 | tf_op jit(solution)/shard_map/all_gather | solution.py:133
  260.8 7.1 %fusion.35 = bf16[1,512,1280]{2,1,0:T(8,128)(2,1)} fusion(bf16[512,2048]{0,1:T(8,128)(2,1)} %all-gather.8.cloned.1.call-done, bf16[2048,1280]{1,0:T(8,128)(2,1)} %param.17, pred[512]{0:T(512)(128)(4,1)S(1)} %iota_compare_fusion.2), kind=kOutput, calls=%fused_computation.47 | convolution fusion | flops 2685665280 | bytes 8651264 | tf_op jit(solution)/shard_map/dot_general | solution.py:132
  (136 shorter events, 70.9 us)
Async XLA Ops:
  6.5 216.0 %copy-start = (bf16[5120,128]{1,0:T(8,128)(2,1)S(1)}, bf16[5120,128]{1,0:T(8,128)(2,1)}, u32[]{:S(2)}) copy-start(bf16[5120,128]{1,0:T(8,128)(2,1)} %param.16) | copy-start | bytes 3932164
  6.5 62.5 %all-gather.6.cloned.1.call-start = ((), (), s32[]{:S(2)}) async-start(), calls=%async_computation.1 | async-start | bytes 6553600 | tf_op jit(solution)/shard_map/all_gather | solution.py:77
  7.3 111.2 %all-gather.4.cloned.1.call-start = ((), (), s32[]{:S(2)}) async-start(), calls=%async_computation | async-start | bytes 4325376 | tf_op jit(solution)/shard_map/all_gather | solution.py:111
  8.0 252.8 %all-gather.8.cloned.1.call-start = ((), (), s32[]{:S(2)}) async-start(), calls=%async_computation.2 | async-start | bytes 2621440 | tf_op jit(solution)/shard_map/all_gather | solution.py:133
  21.6 51.2 %copy-start.2 = (f32[5120]{0:T(1024)S(1)}, f32[5120]{0:T(1024)}, u32[]{:S(2)}) copy-start(f32[5120]{0:T(1024)} %param.13) | copy-start | bytes 61444
  69.0 4.0 %copy-start.1 = (bf16[1,512,5120]{2,1,0:T(8,128)(2,1)S(1)}, bf16[1,512,5120]{2,1,0:T(8,128)(2,1)}, u32[]{:S(2)}) copy-start(bf16[1,512,5120]{2,1,0:T(8,128)(2,1)} %all-gather.6.cloned.1.call-done) | copy-start | bytes 15728644
Sparse Core Ops, SparseCore 0:
  9.0 59.9 all-gather.5
  71.2 47.1 all-gather.3
  231.2 29.5 all-gather.7
where the time goes:
time: 275 us; the launch traced here: 274 us
  waiting for transfers between devices  108 us (39%)
  matrix products  102 us (37%)
  other arithmetic  30.1 us (11%)
  local copies, waits for them, and re-layouts  18.2 us (7%)
  between operations  15.3 us (6%)
    dot_general x17, matrix products, online_block(): jnp.dot(weights.astype(jnp.bfloat16), block_values, preferred_element_typ...  54.4 us
    all_gather x1, waiting for transfers between devices, local(): whole = lax.all_gather(hidden_in, 'head', axis=2, tiled=True)  46.2 us
    all_gather x1, waiting for transfers between devices, local(): piece = lax.all_gather(prefix_cache, 'tok', axis=0, tiled=True)  30.4 us
    dot_general x17, matrix products, online_block(): lax.dot_general(queries, block_keys, (((1,), (1,)), ((), ())), preferred_...  29.7 us
    all_gather x1, waiting for transfers between devices, local(): lax.all_gather(pieces, 'head', axis=1, tiled=True)  29.7 us
    reduce_sum x17, other arithmetic, online_block(): total = total * factor + jnp.sum(weights, axis=1)  24 us
    dot_general x1, local copies, waits for them, and re-layouts, local(): jnp.dot(normed, w_query, preferred_element_type=jnp.float32)  7.81 us
    dot_general x1, matrix products, local(): jnp.dot(lax.all_gather(pieces, 'head', axis=1, tiled=True), w_out, prefer...  7.12 us
  transfers between devices with their start and end apart: 3, of which 3 were waited for; matrix products, arithmetic and copies ran while one was open for 11% of the time, Pallas kernels for 0%

commit v1 on v0

--- a/solution.py
+++ b/solution.py
@@ -9,6 +9,19 @@
 THETA = 100000000.0
 EPS = 1e-05
 NEG = -1e30
+
+
+def gather_around(x, axis, dim):
+    ways = lax.axis_size(axis)
+    up = [(d, (d + 1) % ways) for d in range(ways)]
+    down = [(d, (d - 1) % ways) for d in range(ways)]
+    earlier, later = ([x], [x])
+    for _ in range(ways // 2):
+        earlier.append(lax.ppermute(earlier[-1], axis, up))
+    for _ in range((ways - 1) // 2):
+        later.append(lax.ppermute(later[-1], axis, down))
+    line = jnp.concatenate([*earlier[::-1], *later[1:]], axis=dim)
+    return jnp.roll(line, (lax.axis_index(axis) - ways // 2) * x.shape[dim], axis=dim)
 
 
 def rope_angles(positions, size):
@@ -74,7 +87,7 @@
     request_group,
 ):
     local_len = hidden_in.shape[1]
-    whole = lax.all_gather(hidden_in, "head", axis=2, tiled=True)
+    whole = gather_around(hidden_in, "head", 2)
     flat = whole.reshape(local_len, whole.shape[2]).astype(jnp.float32)
     inverse = lax.rsqrt(jnp.mean(flat * flat, axis=1, keepdims=True) + EPS)
     normed = (flat * inverse * norm_gain[None, :]).astype(jnp.bfloat16)

time: 275 us -> 341 us (1.24)
  matrix products: 102 us -> 147 us
  other arithmetic: 30.1 us -> 68 us
  waiting for transfers between devices: 108 us -> 75.8 us
  local copies, waits for them, and re-layouts: 18.2 us -> 27.6 us
  starting transfers between devices: 0.08 us -> 4.9 us
    all_gather x1 -> x0, waiting for transfers between devices: 46.2 us -> none  [local(): whole = lax.all_gather(hidden_in, 'head', axis=2, tiled=True)]
    ppermute x0 -> x3, waiting for transfers between devices: none -> 43.1 us  [the longest x2 43.1 us: gather_around(): earlier.append(lax.ppermute(earlier[-1], axis, up))]
    reduce_sum x17, other arithmetic: 24 us -> 61.1 us  [online_block(): total = total * factor + jnp.sum(weights, axis=1)]
    dot_general x17, matrix products: 29.7 us -> 61.3 us  [online_block(): lax.dot_general(queries, block_keys, (((1,), (1,)), ((), ())), preferred_...]
    all_gather x1, waiting for transfers between devices: 30.4 us -> 0.01 us  [local(): piece = lax.all_gather(prefix_cache, 'tok', axis=0, tiled=True)]
    dot_general x17, matrix products: 54.4 us -> 69 us  [online_block(): jnp.dot(weights.astype(jnp.bfloat16), block_values, preferred_element_typ...]
    unnamed x6 -> x19, local copies, waits for them, and re-layouts: 0.3 us -> 7.91 us
    ppermute x0 -> x3, starting transfers between devices: none -> 4.86 us  [the longest x1 2.67 us: gather_around(): later.append(lax.ppermute(later[-1], axis, down))]
  transfers between devices with their start and end apart: 3 -> 5, of which waited for: 3 -> 3; matrix products, arithmetic and copies ran while one was open for 11% -> 12% of each run, Pallas kernels for 0% -> 0%
where the time goes in v1:
time: 341 us; the launch traced here: 340 us
  matrix products  147 us (43%)
  waiting for transfers between devices  75.8 us (22%)
  other arithmetic  68 us (20%)
  local copies, waits for them, and re-layouts  27.6 us (8%)
  between operations  15.6 us (5%)
  starting transfers between devices  4.9 us (1%)
    dot_general x17, matrix products, online_block(): jnp.dot(weights.astype(jnp.bfloat16), block_values, preferred_element_typ...  69 us
    dot_general x17, matrix products, online_block(): lax.dot_general(queries, block_keys, (((1,), (1,)), ((), ())), preferred_...  61.3 us
    reduce_sum x17, other arithmetic, online_block(): total = total * factor + jnp.sum(weights, axis=1)  61.1 us
    ppermute x2, waiting for transfers between devices, gather_around(): earlier.append(lax.ppermute(earlier[-1], axis, up))  43.1 us
    all_gather x1, waiting for transfers between devices, local(): lax.all_gather(pieces, 'head', axis=1, tiled=True)  32 us
    dot_general x1, local copies, waits for them, and re-layouts, local(): jnp.dot(normed, w_query, preferred_element_type=jnp.float32)  8.09 us
    unnamed x19, local copies, waits for them, and re-layouts  7.91 us
    dot_general x1, matrix products, local(): jnp.dot(lax.all_gather(pieces, 'head', axis=1, tiled=True), w_out, prefer...  7.12 us
  transfers between devices with their start and end apart: 5, of which 3 were waited for; matrix products, arithmetic and copies ran while one was open for 12% of the time, Pallas kernels for 0%

profile of v1, /device:TPU:1, one launch (start us, length us, event | category | flops | bytes accessed | tf_op | source)
XLA Modules:
  0.0 339.6 jit_solution(5467055903908828194)
XLA Ops:
  9.5 30.1 %collective-permute-done = bf16[1,512,1280]{2,1,0:T(8,128)(2,1)} collective-permute-done((bf16[1,512,1280]{2,1,0:T(8,128)(2,1)}, bf16[1,512,1280]{2,1,0:T(8,128)(2,1)}, u32[]{:S(2)}, u32[]{:S(2)}) %collective-permute-start) | collective-permute-done | bytes 1310752 | tf_op jit(solution)/shard_map/ppermute | solution.py:20
  48.2 8.1 %copy.24 = bf16[512,5120]{1,0:T(8,128)(2,1)} copy(bf16[512,5120]{0,1:T(8,128)(2,1)} %bitcast.66) | data formatting | bytes 10485760 | tf_op jit(solution)/shard_map/dot_general | solution.py:103
  57.1 13.0 %collective-permute-done.1 = bf16[1,512,1280]{2,1,0:T(8,128)(2,1)} collective-permute-done((bf16[1,512,1280]{2,1,0:T(8,128)(2,1)}, bf16[1,512,1280]{2,1,0:T(8,128)(2,1)}, u32[]{:S(2)}, u32[]{:S(2)}) %collective-permute-start.1) | collective-permute-done | bytes 1310752 | tf_op jit(solution)/shard_map/ppermute | solution.py:20
  79.7 4.5 %fusion.21 = f32[512]{0:T(512)S(1)} fusion(bf16[1,512,10240]{2,1,0:T(8,128)(2,1)S(1)} %constant_dynamic-update-slice_fusion, s32[]{:T(128)S(6)} %select_n.52), kind=kLoop, calls=%fused_computation.30 | loop fusion | flops 7863808 | bytes 5244932 | tf_op jit(solution)/shard_map/reduce_sum | solution.py:92
  84.3 3.8 %fusion.27 = f32[512,4,128]{0,2,1:T(8,128)S(1)} fusion(bf16[4,128,5120]{2,1,0:T(8,128)(2,1)S(1)} %bitcast.69, f32[5120]{0:T(1024)S(1)} %copy-done.4, f32[512]{0:T(512)S(1)} %add_rsqrt_fusion, bf16[1,512,10240]{2,1,0:T(8,128)(2,1)S(1)} %constant_dynamic-update-slice_fusion, s32[]{:T(128)S(6)} %select_n.52), kind=kOutput, calls=%fused_computation.36 | convolution fusion | flops 2694840320 | bytes 11556868 | tf_op jit(solution)/shard_map/dot_general | solution.py:103
  88.7 6.1 %convolution_bitcast_fusion = f32[512,1,128]{0,2,1:T(8,128)S(1)} fusion(bf16[5120,128]{1,0:T(8,128)(2,1)} %param.15, f32[5120]{0:T(1024)S(1)} %copy-done.4, f32[512]{0:T(512)S(1)} %add_rsqrt_fusion, bf16[1,512,10240]{2,1,0:T(8,128)(2,1)} %copy-done.3, s32[]{:T(128)S(6)} %select_n.52), kind=kOutput, calls=%fused_computation.55 | convolution fusion | flops 681574400 | bytes 6838276 | tf_op jit(solution)/shard_map/dot_general | solution.py:107
  98.7 4.8 %fusion.69 = (bf16[64,1,128,128]{3,2,1,0:T(8,128)(2,1)}, bf16[64,1,128,128]{3,2,1,0:T(8,128)(2,1)}) fusion(bf16[64,2,128,128]{3,2,1,0:T(8,128)(2,1)} %all-gather.3.cloned.1.call-done), kind=kLoop, calls=%fused_computation.104 | loop fusion | bytes 8388608 | tf_op jit(solution)/shard_map/slice | solution.py:131
  103.5 177.1 %while.15 = (s32[]{:T(128)}, f32[2048]{0:T(1024)S(1)}, f32[2048]{0:T(1024)S(1)}, f32[2048,128]{1,0:T(8,128)}, pred[16,1,512]{2,1,0:T(4,128)(4,1)S(1)}, /*index=5...) while((s32[]{:T(128)}, f32[2048]{0:T(1024)S(1)}, ...), condition=%wide.region_5.6_spmd.clone, body=%wide.region_2.5_spmd.clone.sunk | while | flops 551299072 | bytes 32378512 | solution.py:73
  121.5 3.8 %convolution_add_fusion.3 = f32[2048,128]{1,0:T(8,128)} fusion(f32[512,2048]{1,0:T(8,128)S(1)} %copy-done.1, f32[2048]{0:T(1024)S(1)} %select_maximum_fusion.2, pred[512]{0:T(512)(128)(4,1)S(1)} %dynamic-slice_reduce_fusion.2, f32[2048,128]{1,0:T(8,128)} %get-tuple-element.205, f32[2048]{0:T(1024)S(1)} %get-tuple-element.191, pred[]{:T(512)S(6)} %compare.4, ...), kind=kOutput, calls=%fused_computation.5.clone.1 | convolution fusion | flops 274464768 | bytes 6439937 | tf_op jit(solution)/shard_map/while/body/eval_jaxpr/dot_general | solution.py:54
  132.6 3.8 %convolution_add_fusion.3 = f32[2048,128]{1,0:T(8,128)} fusion(f32[512,2048]{1,0:T(8,128)S(1)} %copy-done.1, f32[2048]{0:T(1024)S(1)} %select_maximum_fusion.2, pred[512]{0:T(512)(128)(4,1)S(1)} %dynamic-slice_reduce_fusion.2, f32[2048,128]{1,0:T(8,128)} %get-tuple-element.205, f32[2048]{0:T(1024)S(1)} %get-tuple-element.191, pred[]{:T(512)S(6)} %compare.4, ...), kind=kOutput, calls=%fused_computation.5.clone.1 | convolution fusion | flops 274464768 | bytes 6439937 | tf_op jit(solution)/shard_map/while/body/eval_jaxpr/dot_general | solution.py:54
  143.7 3.8 %convolution_add_fusion.3 = f32[2048,128]{1,0:T(8,128)} fusion(f32[512,2048]{1,0:T(8,128)S(1)} %copy-done.1, f32[2048]{0:T(1024)S(1)} %select_maximum_fusion.2, pred[512]{0:T(512)(128)(4,1)S(1)} %dynamic-slice_reduce_fusion.2, f32[2048,128]{1,0:T(8,128)} %get-tuple-element.205, f32[2048]{0:T(1024)S(1)} %get-tuple-element.191, pred[]{:T(512)S(6)} %compare.4, ...), kind=kOutput, calls=%fused_computation.5.clone.1 | convolution fusion | flops 274464768 | bytes 6439937 | tf_op jit(solution)/shard_map/while/body/eval_jaxpr/dot_general | solution.py:54
  154.8 3.8 %convolution_add_fusion.3 = f32[2048,128]{1,0:T(8,128)} fusion(f32[512,2048]{1,0:T(8,128)S(1)} %copy-done.1, f32[2048]{0:T(1024)S(1)} %select_maximum_fusion.2, pred[512]{0:T(512)(128)(4,1)S(1)} %dynamic-slice_reduce_fusion.2, f32[2048,128]{1,0:T(8,128)} %get-tuple-element.205, f32[2048]{0:T(1024)S(1)} %get-tuple-element.191, pred[]{:T(512)S(6)} %compare.4, ...), kind=kOutput, calls=%fused_computation.5.clone.1 | convolution fusion | flops 274464768 | bytes 6439937 | tf_op jit(solution)/shard_map/while/body/eval_jaxpr/dot_general | solution.py:54
  165.8 3.8 %convolution_add_fusion.3 = f32[2048,128]{1,0:T(8,128)} fusion(f32[512,2048]{1,0:T(8,128)S(1)} %copy-done.1, f32[2048]{0:T(1024)S(1)} %select_maximum_fusion.2, pred[512]{0:T(512)(128)(4,1)S(1)} %dynamic-slice_reduce_fusion.2, f32[2048,128]{1,0:T(8,128)} %get-tuple-element.205, f32[2048]{0:T(1024)S(1)} %get-tuple-element.191, pred[]{:T(512)S(6)} %compare.4, ...), kind=kOutput, calls=%fused_computation.5.clone.1 | convolution fusion | flops 274464768 | bytes 6439937 | tf_op jit(solution)/shard_map/while/body/eval_jaxpr/dot_general | solution.py:54
  176.9 3.8 %convolution_add_fusion.3 = f32[2048,128]{1,0:T(8,128)} fusion(f32[512,2048]{1,0:T(8,128)S(1)} %copy-done.1, f32[2048]{0:T(1024)S(1)} %select_maximum_fusion.2, pred[512]{0:T(512)(128)(4,1)S(1)} %dynamic-slice_reduce_fusion.2, f32[2048,128]{1,0:T(8,128)} %get-tuple-element.205, f32[2048]{0:T(1024)S(1)} %get-tuple-element.191, pred[]{:T(512)S(6)} %compare.4, ...), kind=kOutput, calls=%fused_computation.5.clone.1 | convolution fusion | flops 274464768 | bytes 6439937 | tf_op jit(solution)/shard_map/while/body/eval_jaxpr/dot_general | solution.py:54
  188.0 3.8 %convolution_add_fusion.3 = f32[2048,128]{1,0:T(8,128)} fusion(f32[512,2048]{1,0:T(8,128)S(1)} %copy-done.1, f32[2048]{0:T(1024)S(1)} %select_maximum_fusion.2, pred[512]{0:T(512)(128)(4,1)S(1)} %dynamic-slice_reduce_fusion.2, f32[2048,128]{1,0:T(8,128)} %get-tuple-element.205, f32[2048]{0:T(1024)S(1)} %get-tuple-element.191, pred[]{:T(512)S(6)} %compare.4, ...), kind=kOutput, calls=%fused_computation.5.clone.1 | convolution fusion | flops 274464768 | bytes 6439937 | tf_op jit(solution)/shard_map/while/body/eval_jaxpr/dot_general | solution.py:54
  210.2 3.8 %convolution_add_fusion.3 = f32[2048,128]{1,0:T(8,128)} fusion(f32[512,2048]{1,0:T(8,128)S(1)} %copy-done.1, f32[2048]{0:T(1024)S(1)} %select_maximum_fusion.2, pred[512]{0:T(512)(128)(4,1)S(1)} %dynamic-slice_reduce_fusion.2, f32[2048,128]{1,0:T(8,128)} %get-tuple-element.205, f32[2048]{0:T(1024)S(1)} %get-tuple-element.191, pred[]{:T(512)S(6)} %compare.4, ...), kind=kOutput, calls=%fused_computation.5.clone.1 | convolution fusion | flops 274464768 | bytes 6439937 | tf_op jit(solution)/shard_map/while/body/eval_jaxpr/dot_general | solution.py:54
  221.3 3.8 %convolution_add_fusion.3 = f32[2048,128]{1,0:T(8,128)} fusion(f32[512,2048]{1,0:T(8,128)S(1)} %copy-done.1, f32[2048]{0:T(1024)S(1)} %select_maximum_fusion.2, pred[512]{0:T(512)(128)(4,1)S(1)} %dynamic-slice_reduce_fusion.2, f32[2048,128]{1,0:T(8,128)} %get-tuple-element.205, f32[2048]{0:T(1024)S(1)} %get-tuple-element.191, pred[]{:T(512)S(6)} %compare.4, ...), kind=kOutput, calls=%fused_computation.5.clone.1 | convolution fusion | flops 274464768 | bytes 6439937 | tf_op jit(solution)/shard_map/while/body/eval_jaxpr/dot_general | solution.py:54
  243.5 3.8 %convolution_add_fusion.3 = f32[2048,128]{1,0:T(8,128)} fusion(f32[512,2048]{1,0:T(8,128)S(1)} %copy-done.1, f32[2048]{0:T(1024)S(1)} %select_maximum_fusion.2, pred[512]{0:T(512)(128)(4,1)S(1)} %dynamic-slice_reduce_fusion.2, f32[2048,128]{1,0:T(8,128)} %get-tuple-element.205, f32[2048]{0:T(1024)S(1)} %get-tuple-element.191, pred[]{:T(512)S(6)} %compare.4, ...), kind=kOutput, calls=%fused_computation.5.clone.1 | convolution fusion | flops 274464768 | bytes 6439937 | tf_op jit(solution)/shard_map/while/body/eval_jaxpr/dot_general | solution.py:54
  254.6 3.8 %convolution_add_fusion.3 = f32[2048,128]{1,0:T(8,128)} fusion(f32[512,2048]{1,0:T(8,128)S(1)} %copy-done.1, f32[2048]{0:T(1024)S(1)} %select_maximum_fusion.2, pred[512]{0:T(512)(128)(4,1)S(1)} %dynamic-slice_reduce_fusion.2, f32[2048,128]{1,0:T(8,128)} %get-tuple-element.205, f32[2048]{0:T(1024)S(1)} %get-tuple-element.191, pred[]{:T(512)S(6)} %compare.4, ...), kind=kOutput, calls=%fused_computation.5.clone.1 | convolution fusion | flops 274464768 | bytes 6439937 | tf_op jit(solution)/shard_map/while/body/eval_jaxpr/dot_general | solution.py:54
  265.7 3.8 %convolution_add_fusion.3 = f32[2048,128]{1,0:T(8,128)} fusion(f32[512,2048]{1,0:T(8,128)S(1)} %copy-done.1, f32[2048]{0:T(1024)S(1)} %select_maximum_fusion.2, pred[512]{0:T(512)(128)(4,1)S(1)} %dynamic-slice_reduce_fusion.2, f32[2048,128]{1,0:T(8,128)} %get-tuple-element.205, f32[2048]{0:T(1024)S(1)} %get-tuple-element.191, pred[]{:T(512)S(6)} %compare.4, ...), kind=kOutput, calls=%fused_computation.5.clone.1 | convolution fusion | flops 274464768 | bytes 6439937 | tf_op jit(solution)/shard_map/while/body/eval_jaxpr/dot_general | solution.py:54
  276.8 3.8 %convolution_add_fusion.3 = f32[2048,128]{1,0:T(8,128)} fusion(f32[512,2048]{1,0:T(8,128)S(1)} %copy-done.1, f32[2048]{0:T(1024)S(1)} %select_maximum_fusion.2, pred[512]{0:T(512)(128)(4,1)S(1)} %dynamic-slice_reduce_fusion.2, f32[2048,128]{1,0:T(8,128)} %get-tuple-element.205, f32[2048]{0:T(1024)S(1)} %get-tuple-element.191, pred[]{:T(512)S(6)} %compare.4, ...), kind=kOutput, calls=%fused_computation.5.clone.1 | convolution fusion | flops 274464768 | bytes 6439937 | tf_op jit(solution)/shard_map/while/body/eval_jaxpr/dot_general | solution.py:54
  284.2 8.5 %fusion.38 = bf16[2048,128]{1,0:T(8,128)(2,1)S(1)} fusion(f32[2048,512]{0,1:T(8,128)} %get-tuple-element.134, f32[2048]{0:T(1024)S(1)} %max.6, s32[2048]{0:T(1024)S(1)} %add_select_fusion, pred[512]{0:T(512)(128)(4,1)S(1)} %iota_compare_fusion.2, f32[2048,128]{1,0:T(8,128)} %get-tuple-element.49, f32[2048]{0:T(1024)S(1)} %get-tuple-element.121, ...), kind=kOutput, calls=%fused_computation.51 | convolution fusion | flops 956366848 | bytes 12376580 | tf_op jit(solution)/shard_map/dot_general | solution.py:54
  293.7 32.0 %all-gather.5.cloned.1.call-done = bf16[512,2048]{0,1:T(8,128)(2,1)} async-done(((bf16[512,512]{0,1:T(8,128)(2,1)}), bf16[512,2048]{0,1:T(8,128)(2,1)}) %all-gather.5.cloned.1.call-update) | async-done | bytes 2097168 | tf_op jit(solution)/shard_map/all_gather | solution.py:146
  325.7 7.1 %fusion.36 = bf16[1,512,1280]{2,1,0:T(8,128)(2,1)} fusion(bf16[512,2048]{0,1:T(8,128)(2,1)} %all-gather.5.cloned.1.call-done, bf16[2048,1280]{1,0:T(8,128)(2,1)} %param.17, pred[512]{0:T(512)(128)(4,1)S(1)} %iota_compare_fusion.2), kind=kOutput, calls=%fused_computation.48 | convolution fusion | flops 2685665280 | bytes 8651264 | tf_op jit(solution)/shard_map/dot_general | solution.py:145
  (186 shorter events, 156.1 us)
Async XLA Ops:
  6.5 277.6 %copy-start = (bf16[5120,128]{1,0:T(8,128)(2,1)S(1)}, bf16[5120,128]{1,0:T(8,128)(2,1)}, u32[]{:S(2)}) copy-start(bf16[5120,128]{1,0:T(8,128)(2,1)} %param.16) | copy-start | bytes 3932164
  6.5 92.2 %all-gather.3.cloned.1.call-start = ((), (), s32[]{:S(2)}) async-start(), calls=%async_computation | async-start | bytes 4325376 | tf_op jit(solution)/shard_map/all_gather | solution.py:124
  7.3 318.4 %all-gather.5.cloned.1.call-start = ((), (), s32[]{:S(2)}) async-start(), calls=%async_computation.1 | async-start | bytes 2621440 | tf_op jit(solution)/shard_map/all_gather | solution.py:146
  7.3 32.3 %collective-permute-start = (bf16[1,512,1280]{2,1,0:T(8,128)(2,1)}, bf16[1,512,1280]{2,1,0:T(8,128)(2,1)}, u32[]{:S(2)}, u32[]{:S(2)}) collective-permute-start(bf16[1,512,1280]{2,1,0:T(8,128)(2,1)} %param.12), channel_id=1, source_target_pairs={{0,1},{1,2},{2,3},{3,0},{4,5},{5,6},{6,7},{7,4},{8,9},{9,10},{10,1... | collective-permute-start | bytes 3932168 | tf_op jit(solution)/shard_map/ppermute | solution.py:20
  39.6 30.5 %collective-permute-start.1 = (bf16[1,512,1280]{2,1,0:T(8,128)(2,1)}, bf16[1,512,1280]{2,1,0:T(8,128)(2,1)}, u32[]{:S(2)}, u32[]{:S(2)}) collective-permute-start(bf16[1,512,1280]{2,1,0:T(8,128)(2,1)} %collective-permute-done), channel_id=1, source_target_pairs={{0,1},{1,2},{2,3},{3,0},{4,5},{5,6},{6,7},{7,4},{8,9},{9,10},{10,1... | collective-permute-start | bytes 3932168 | tf_op jit(solution)/shard_map/ppermute | solution.py:20
  39.6 33.7 %collective-permute-start.2 = (bf16[1,512,1280]{2,1,0:T(8,128)(2,1)}, bf16[1,512,1280]{2,1,0:T(8,128)(2,1)}, u32[]{:S(2)}, u32[]{:S(2)}) collective-permute-start(bf16[1,512,1280]{2,1,0:T(8,128)(2,1)} %param.12), channel_id=1, source_target_pairs={{0,3},{1,0},{2,1},{3,2},{4,7},{5,4},{6,5},{7,6},{8,11},{9,8},{10,9... | collective-permute-start | bytes 3932168 | tf_op jit(solution)/shard_map/ppermute | solution.py:22
  56.3 16.8 %copy-start.2 = (bf16[1,512,1280]{2,1,0:T(8,128)(2,1)S(1)}, bf16[1,512,1280]{2,1,0:T(8,128)(2,1)}, u32[]{:S(2)}) copy-start(bf16[1,512,1280]{2,1,0:T(8,128)(2,1)} %param.12) | copy-start | bytes 3932164
  76.3 8.0 %slice-start = ((s8[5242880]{0:T(1024)(128)(4,1)}), s8[4194304]{0:T(1024)(128)(4,1)S(1)}, s32[]{:S(2)}) async-start(s8[5242880]{0:T(1024)(128)(4,1)} %bitcast.67), calls=%async_computation.2 | async-start | bytes 8388608
  78.1 6.2 %slice-start.1 = ((s8[5242880]{0:T(1024)(128)(4,1)}), s8[1048576]{0:T(1024)(128)(4,1)S(1)}, s32[]{:S(2)}) async-start(s8[5242880]{0:T(1024)(128)(4,1)} %bitcast.67), calls=%async_computation.3 | async-start | bytes 2097152
  78.1 6.2 %copy-start.4 = (f32[5120]{0:T(1024)S(1)}, f32[5120]{0:T(1024)}, u32[]{:S(2)}) copy-start(f32[5120]{0:T(1024)} %param.13) | copy-start | bytes 61444
  79.7 8.4 %copy-start.3 = (bf16[1,512,10240]{2,1,0:T(8,128)(2,1)}, bf16[1,512,10240]{2,1,0:T(8,128)(2,1)S(1)}, u32[]{:S(2)}) copy-start(bf16[1,512,10240]{2,1,0:T(8,128)(2,1)S(1)} %constant_dynamic-update-slice_fusion) | copy-start | bytes 31457284
  107.2 3.6 %copy-start.1 = (f32[512,2048]{1,0:T(8,128)S(1)}, f32[512,2048]{1,0:T(8,128)}, u32[]{:S(2)}) copy-start(f32[512,2048]{1,0:T(8,128)} %get-tuple-element.189) | copy-start | bytes 12582916 | tf_op jit(solution)/shard_map/while
  117.9 3.6 %copy-start.1 = (f32[512,2048]{1,0:T(8,128)S(1)}, f32[512,2048]{1,0:T(8,128)}, u32[]{:S(2)}) copy-start(f32[512,2048]{1,0:T(8,128)} %get-tuple-element.189) | copy-start | bytes 12582916 | tf_op jit(solution)/shard_map/while
  128.9 3.6 %copy-start.1 = (f32[512,2048]{1,0:T(8,128)S(1)}, f32[512,2048]{1,0:T(8,128)}, u32[]{:S(2)}) copy-start(f32[512,2048]{1,0:T(8,128)} %get-tuple-element.189) | copy-start | bytes 12582916 | tf_op jit(solution)/shard_map/while
  140.0 3.6 %copy-start.1 = (f32[512,2048]{1,0:T(8,128)S(1)}, f32[512,2048]{1,0:T(8,128)}, u32[]{:S(2)}) copy-start(f32[512,2048]{1,0:T(8,128)} %get-tuple-element.189) | copy-start | bytes 12582916 | tf_op jit(solution)/shard_map/while
  151.1 3.6 %copy-start.1 = (f32[512,2048]{1,0:T(8,128)S(1)}, f32[512,2048]{1,0:T(8,128)}, u32[]{:S(2)}) copy-start(f32[512,2048]{1,0:T(8,128)} %get-tuple-element.189) | copy-start | bytes 12582916 | tf_op jit(solution)/shard_map/while
  162.2 3.6 %copy-start.1 = (f32[512,2048]{1,0:T(8,128)S(1)}, f32[512,2048]{1,0:T(8,128)}, u32[]{:S(2)}) copy-start(f32[512,2048]{1,0:T(8,128)} %get-tuple-element.189) | copy-start | bytes 12582916 | tf_op jit(solution)/shard_map/while
  173.3 3.6 %copy-start.1 = (f32[512,2048]{1,0:T(8,128)S(1)}, f32[512,2048]{1,0:T(8,128)}, u32[]{:S(2)}) copy-start(f32[512,2048]{1,0:T(8,128)} %get-tuple-element.189) | copy-start | bytes 12582916 | tf_op jit(solution)/shard_map/while
  184.4 3.6 %copy-start.1 = (f32[512,2048]{1,0:T(8,128)S(1)}, f32[512,2048]{1,0:T(8,128)}, u32[]{:S(2)}) copy-start(f32[512,2048]{1,0:T(8,128)} %get-tuple-element.189) | copy-start | bytes 12582916 | tf_op jit(solution)/shard_map/while
  195.5 3.6 %copy-start.1 = (f32[512,2048]{1,0:T(8,128)S(1)}, f32[512,2048]{1,0:T(8,128)}, u32[]{:S(2)}) copy-start(f32[512,2048]{1,0:T(8,128)} %get-tuple-element.189) | copy-start | bytes 12582916 | tf_op jit(solution)/shard_map/while
  206.6 3.6 %copy-start.1 = (f32[512,2048]{1,0:T(8,128)S(1)}, f32[512,2048]{1,0:T(8,128)}, u32[]{:S(2)}) copy-start(f32[512,2048]{1,0:T(8,128)} %get-tuple-element.189) | copy-start | bytes 12582916 | tf_op jit(solution)/shard_map/while
  217.7 3.6 %copy-start.1 = (f32[512,2048]{1,0:T(8,128)S(1)}, f32[512,2048]{1,0:T(8,128)}, u32[]{:S(2)}) copy-start(f32[512,2048]{1,0:T(8,128)} %get-tuple-element.189) | copy-start | bytes 12582916 | tf_op jit(solution)/shard_map/while
  228.8 3.6 %copy-start.1 = (f32[512,2048]{1,0:T(8,128)S(1)}, f32[512,2048]{1,0:T(8,128)}, u32[]{:S(2)}) copy-start(f32[512,2048]{1,0:T(8,128)} %get-tuple-element.189) | copy-start | bytes 12582916 | tf_op jit(solution)/shard_map/while
  262.0 3.6 %copy-start.1 = (f32[512,2048]{1,0:T(8,128)S(1)}, f32[512,2048]{1,0:T(8,128)}, u32[]{:S(2)}) copy-start(f32[512,2048]{1,0:T(8,128)} %get-tuple-element.189) | copy-start | bytes 12582916 | tf_op jit(solution)/shard_map/while
  (3 other events, 10.9 us)
Sparse Core Ops, SparseCore 0:
  9.6 49.7 all-gather.2
  293.8 31.7 all-gather.4
